TPU v7x, 512 devices: a whole 4x8x8 slice. The times are simulated.
512 devices in a mesh: shift: 4 (over x_hi, core), space: 128 (over y, z, x_lo).
Axes of the slice: x: 4 (x_hi: 2, x_lo: 2; x = x_hi * 2 + x_lo), y: 8, z: 8, core: 2. Of those that a mesh axis runs over, the one named last changes fastest.
Arguments:
- labels: int32 [256, 32, 256], P('space'), may hold values from 0 to 7
- conductance: float32 [8], replicated, may hold values from 0.2 to 5
- capacity_table: float32 [8], replicated, may hold values from 0.5 to 2
- shift_values: float32 [8], replicated, may hold values from 0.1 to 4
- prior_basis: float32 [256, 256, 32, 256], P(None, 'space', 'shift'), may hold values from -6 to 6
Outputs:
- new_block: float32 [8, 8, 256, 32, 256], P(None, None, 'space', 'shift')
- coefficients: float32 [64, 256], replicated
- factor: float32 [64, 64], replicated
All inputs are finite; a program needn't handle non-finite values.
Results may differ from a plain program's by a relative error of at most 0.0003.
Values sent between devices are 32-bit elements; how exact they have to be, the bound alone decides.
No kernel may reach another device: no remote copies, remote signals or barrier semaphores. Data moves between devices by JAX's collectives and lax.ppermute only.
A program may use at most 64 MiB of HBM per device.

v0:
```python
import jax
import jax.numpy as jnp
from jax import lax
from jax.sharding import PartitionSpec as P

COLS = 8
SWEEPS = 4
LOWER_BOUND = 0.1
UPPER_BOUND = 2.0


def padded_2(cells, sides, width):
    for axis, dim in sides:
        count = lax.axis_size(axis)
        ends = count - 1
        head = lax.slice_in_dim(cells, 0, width, axis=dim)
        tail = lax.slice_in_dim(cells, cells.shape[dim] - width, cells.shape[dim], axis=dim)
        cells = jnp.concatenate(
            [
                lax.ppermute(tail, axis, [(i, (i + 1) % count) for i in range(ends)]),
                cells,
                lax.ppermute(head, axis, [((i + 1) % count, i) for i in range(ends)]),
            ],
            axis=dim,
        )
    return cells


def lookup(labels, table):
    materials = jnp.arange(table.shape[0], dtype=jnp.int32)
    onehot = (labels[None] == materials[:, None, None, None]).astype(jnp.float32)
    return jnp.sum(onehot * table[:, None, None, None], axis=0)


def conductances(conduct, padded):
    west_face = 0.5 * (conduct + padded[:-2, 1:-1, 1:-1])
    east_face = 0.5 * (conduct + padded[2:, 1:-1, 1:-1])
    south_face = 0.5 * (conduct + padded[1:-1, :-2, 1:-1])
    north_face = 0.5 * (conduct + padded[1:-1, 2:, 1:-1])
    below_face = 0.5 * (conduct + padded[1:-1, 1:-1, :-2])
    above_face = 0.5 * (conduct + padded[1:-1, 1:-1, 2:])
    return (west_face, east_face, south_face, north_face, below_face, above_face)


def neighbours(padded, face_list):
    west_face, east_face, south_face, north_face, below_face, above_face = face_list
    summed = west_face * padded[..., :-2, 1:-1, 1:-1] + east_face * padded[..., 2:, 1:-1, 1:-1]
    summed = (
        summed
        + south_face * padded[..., 1:-1, :-2, 1:-1]
        + north_face * padded[..., 1:-1, 2:, 1:-1]
    )
    summed = (
        summed
        + below_face * padded[..., 1:-1, 1:-1, :-2]
        + above_face * padded[..., 1:-1, 1:-1, 2:]
    )
    return summed


def diagonal_of(face_list, shift_list, capacity):
    west_face, east_face, south_face, north_face, below_face, above_face = face_list
    summed = west_face + east_face + (south_face + north_face) + (below_face + above_face)
    return summed[None, None] + shift_list[:, None, None, None, None] * capacity[None, None]


def chebyshev(source, face_list, diagonal, padder):
    center = 0.5 * (UPPER_BOUND + LOWER_BOUND)
    spread = 0.5 * (UPPER_BOUND - LOWER_BOUND)
    ratio_value = center / spread
    reciprocal = 1.0 / diagonal
    solution = jnp.zeros_like(source)
    remainder = source
    weight_old = 1.0 / ratio_value
    direction = reciprocal * remainder / center
    for sweep_index in range(SWEEPS):
        solution = solution + direction
        if sweep_index + 1 < SWEEPS:
            applied = diagonal * direction - neighbours(padder(direction), face_list)
            remainder = remainder - applied
            weight_new = 1.0 / (2.0 * ratio_value - weight_old)
            direction = weight_new * weight_old * direction + 2.0 * weight_new / spread * (
                reciprocal * remainder
            )
            weight_old = weight_new
    return solution


def products(left_side, right_side):
    return lax.dot_general(
        left_side, right_side, (((1,), (1,)), ((), ())), precision=lax.Precision.HIGHEST
    )


def matmul(left_side, right_side):
    return jnp.dot(left_side, right_side, precision=lax.Precision.HIGHEST)


def local(labels, conductance, capacity_table, shift_values, prior_basis):
    groups = lax.axis_size("shift")
    shifts_all = shift_values.shape[0]
    per_device = shifts_all // groups
    new_count = shifts_all * COLS
    basis_count = prior_basis.shape[0]
    slab_x = prior_basis.shape[1]
    quarter = prior_basis.shape[2]
    depth = prior_basis.shape[3]
    flat_basis = prior_basis.reshape(basis_count, slab_x * quarter * depth)
    cell_weight = 1.0 / (slab_x * quarter * depth * groups * lax.axis_size("space"))
    tail_columns = prior_basis[basis_count - new_count :]
    conduct = lookup(labels, conductance)
    capacity = lookup(labels, capacity_table)
    rimmed = padded_2(conduct, (("space", 0),), 1)
    face_list = conductances(conduct, jnp.pad(rimmed, ((0, 0), (1, 1), (1, 1))))
    shift_list = lax.dynamic_slice_in_dim(
        shift_values, lax.axis_index("shift") * per_device, per_device, 0
    )
    diagonal = diagonal_of(face_list, shift_list, capacity)
    starting = lax.all_to_all(tail_columns, "shift", split_axis=0, concat_axis=2, tiled=True)
    full_y = starting.shape[2]
    source = starting.reshape(per_device, COLS, slab_x, full_y, depth) * capacity[None, None]

    def padder(field):
        widened = padded_2(field, (("space", 2),), 1)
        return jnp.pad(widened, ((0, 0), (0, 0), (0, 0), (1, 1), (1, 1)))

    fields = chebyshev(source, face_list, diagonal, padder)
    merged = fields.reshape(per_device * COLS, slab_x, full_y, depth)
    regrouped = lax.all_to_all(merged, "shift", split_axis=2, concat_axis=0, tiled=True)
    columns = regrouped.reshape(new_count, slab_x * quarter * depth)
    first_proj = lax.psum(products(columns, flat_basis), ("shift", "space")) * cell_weight
    columns = columns - matmul(first_proj, flat_basis)
    second_proj = lax.psum(products(columns, flat_basis), ("shift", "space")) * cell_weight
    columns = columns - matmul(second_proj, flat_basis)
    gram_matrix = lax.psum(products(columns, columns), ("shift", "space")) * cell_weight
    factor = jnp.linalg.cholesky(gram_matrix)
    orthonormal = lax.linalg.triangular_solve(factor, columns, left_side=True, lower=True)
    new_block = orthonormal.reshape(shifts_all, COLS, slab_x, quarter, depth)
    return (new_block, first_proj + second_proj, factor)


def solution(mesh):
    in_specs = (P("space", None, None), P(), P(), P(), P(None, "space", "shift", None))
    out_specs = (P(None, None, "space", "shift", None), P(), P())
    return jax.shard_map(local, mesh=mesh, in_specs=in_specs, out_specs=out_specs, check_vma=False)
```

profile of v0, /device:TPU:1, one launch (start us, length us, event | category | flops | bytes accessed | tf_op | source)
XLA Modules:
  0.0 803.1 jit_solution(15233755541338323633)
XLA Ops:
  7.2 2.3 slice.133
  9.5 10.4 %all-to-all-start = ((f32[64,2,8,256]{3,2,1,0:T(8,128)}), f32[64,2,8,256]{3,2,1,0:T(8,128)S(1)}, u32[]{:S(2)}, u32[]{:S(2)}) async-start(f32[64,2,8,256]{3,2,1,0:T(8,128)} %slice.133), calls=%async_computation | async-start | bytes 2097152 | tf_op jit(solution)/shard_map/all_to_all | solution.py:119
  22.8 10.3 %collective-permute-done = f32[1,32,256]{2,1,0:T(8,128)S(1)} collective-permute-done((f32[1,32,256]{2,1,0:T(8,128)S(1)}, f32[1,32,256]{2,1,0:T(8,128)S(1)}, u32[]{:S(2)}, u32[]{:S(2)}) %collective-permute-start) | collective-permute-done | bytes 32800 | tf_op jit(solution)/shard_map/ppermute | solution.py:20
  33.4 2.3 all-to-all-done
  36.1 1.9 collective-permute-start.2
  39.2 20.6 %collective-permute-done.2 = f32[2,8,1,32,256]{4,3,2,1,0:T(8,128)S(1)} collective-permute-done((f32[2,8,1,32,256]{4,3,2,1,0:T(8,128)S(1)}, f32[2,8,1,32,256]{4,3,2,1,0:T(8,128)S(1)}, u32[]{:S(2)}, u32[]{:S(2)}) %collective-permute-start.2) | collective-permute-done | bytes 524320 | tf_op jit(solution)/shard_map/ppermute | solution.py:20
  59.8 1.8 select_maximum_fusion.4
  62.9 4.1 collective-permute-start.4
  68.4 19.6 %collective-permute-done.4 = f32[2,8,1,32,256]{4,3,2,1,0:T(8,128)S(1)} collective-permute-done((f32[2,8,1,32,256]{4,3,2,1,0:T(8,128)S(1)}, f32[2,8,1,32,256]{4,3,2,1,0:T(8,128)S(1)}, u32[]{:S(2)}, u32[]{:S(2)}) %collective-permute-start.4) | collective-permute-done | bytes 524320 | tf_op jit(solution)/shard_map/ppermute | solution.py:20
  88.0 1.8 select_maximum_fusion.2
  91.1 4.1 collective-permute-start.6
  96.6 18.6 %collective-permute-done.6 = f32[2,8,1,32,256]{4,3,2,1,0:T(8,128)S(1)} collective-permute-done((f32[2,8,1,32,256]{4,3,2,1,0:T(8,128)S(1)}, f32[2,8,1,32,256]{4,3,2,1,0:T(8,128)S(1)}, u32[]{:S(2)}, u32[]{:S(2)}) %collective-permute-start.6) | collective-permute-done | bytes 524320 | tf_op jit(solution)/shard_map/ppermute | solution.py:20
  120.1 6.9 all-to-all-start.1
  127.0 7.9 copy.46
  135.0 7.2 all-to-all-done.1
  143.1 6.8 fusion.71
  150.2 267.6 %all-reduce.7.cloned.1.call-done = f32[64,256]{1,0:T(8,128)} async-done(((f32[64,256]{1,0:T(8,128)}), f32[64,256]{1,0:T(8,128)}) %all-reduce.7.cloned.1.call-update) | async-done | bytes 65552 | tf_op jit(solution)/shard_map/psum | solution.py:131
  417.8 5.0 convolution_subtract_fusion.1
  422.7 4.6 fusion.72
  427.4 251.4 %all-reduce.9.cloned.1.call-done = f32[64,256]{1,0:T(8,128)} async-done(((f32[64,256]{1,0:T(8,128)}), f32[64,256]{1,0:T(8,128)}) %all-reduce.9.cloned.1.call-update) | async-done | bytes 65552 | tf_op jit(solution)/shard_map/psum | solution.py:133
  678.8 4.8 convolution_subtract_fusion
  684.6 94.9 %psum.23 = f32[64,64]{0,1:T(8,128)S(1)} all-reduce(f32[64,64]{0,1:T(8,128)S(1)} %fusion.73), channel_id=1, replica_groups=mesh['shift'=4,'space'=128] {'shift','space'}, use_global_device_ids=true, to_apply=%region_4.5 | all-reduce | flops 4096 | bytes 32768 | tf_op jit(solution)/shard_map/psum | solution.py:135
  779.6 5.8 cholesky.16
  787.4 4.9 custom-call.6
  (58 shorter events, 23.2 us)
Async XLA Ops:
  7.2 12.7 %copy-start.5 = (f32[8]{0:T(128)S(1)}, f32[8]{0:T(128)}, u32[]{:S(2)}) copy-start(f32[8]{0:T(128)} %param.7) | copy-start | bytes 100
  7.2 12.7 %copy-start.4 = (f32[8]{0:T(128)S(1)}, f32[8]{0:T(128)}, u32[]{:S(2)}) copy-start(f32[8]{0:T(128)} %param.6) | copy-start | bytes 100
  7.2 12.7 %copy-start.3 = (s32[2,32,256]{2,1,0:T(8,128)S(1)}, s32[2,32,256]{2,1,0:T(8,128)}, u32[]{:S(2)}) copy-start(s32[2,32,256]{2,1,0:T(8,128)} %param.5) | copy-start | bytes 196612
  7.2 15.5 %copy-start.6 = (f32[8]{0:T(128)S(1)}, f32[8]{0:T(128)}, u32[]{:S(2)}) copy-start(f32[8]{0:T(128)} %param.8) | copy-start | bytes 100
  9.5 26.2 %all-to-all-start = ((f32[64,2,8,256]{3,2,1,0:T(8,128)}), f32[64,2,8,256]{3,2,1,0:T(8,128)S(1)}, u32[]{:S(2)}, u32[]{:S(2)}) async-start(f32[64,2,8,256]{3,2,1,0:T(8,128)} %slice.133), calls=%async_computation | async-start | bytes 2097152 | tf_op jit(solution)/shard_map/all_to_all | solution.py:119
  20.1 13.0 %collective-permute-start = (f32[1,32,256]{2,1,0:T(8,128)S(1)}, f32[1,32,256]{2,1,0:T(8,128)S(1)}, u32[]{:S(2)}, u32[]{:S(2)}) collective-permute-start(f32[1,32,256]{2,1,0:T(8,128)S(1)} %get-tuple-element.42), channel_id=1, source_target_pairs={{0,1},{1,2},{2,3},{3,4},{4,5},{5,6},{6,7},{7,8},{8,9},{9,10},{10,1... | collective-permute-start | bytes 98312 | tf_op jit(solution)/shard_map/ppermute | solution.py:20
  21.4 11.7 %collective-permute-start.1 = (f32[1,32,256]{2,1,0:T(8,128)S(1)}, f32[1,32,256]{2,1,0:T(8,128)S(1)}, u32[]{:S(2)}, u32[]{:S(2)}) collective-permute-start(f32[1,32,256]{2,1,0:T(8,128)S(1)} %get-tuple-element.43), channel_id=1, source_target_pairs={{1,0},{2,1},{3,2},{4,3},{5,4},{6,5},{7,6},{8,7},{9,8},{10,9},{11,1... | collective-permute-start | bytes 98312 | tf_op jit(solution)/shard_map/ppermute | solution.py:22
  36.1 23.7 %collective-permute-start.2 = (f32[2,8,1,32,256]{4,3,2,1,0:T(8,128)S(1)}, f32[2,8,1,32,256]{4,3,2,1,0:T(8,128)S(1)}, u32[]{:S(2)}, u32[]{:S(2)}) collective-permute-start(f32[2,8,1,32,256]{4,3,2,1,0:T(8,128)S(1)} %get-tuple-element.37), channel_id=1, source_target_pairs={{0,1},{1,2},{2,3},{3,4},{4,5},{5,6},{6,7},{7,8},{8,9},{9,10},{10,1... | collective-permute-start | bytes 1572872 | tf_op jit(solution)/shard_map/ppermute | solution.py:20
  37.9 21.9 %collective-permute-start.3 = (f32[2,8,1,32,256]{4,3,2,1,0:T(8,128)S(1)}, f32[2,8,1,32,256]{4,3,2,1,0:T(8,128)S(1)}, u32[]{:S(2)}, u32[]{:S(2)}) collective-permute-start(f32[2,8,1,32,256]{4,3,2,1,0:T(8,128)S(1)} %get-tuple-element.38), channel_id=1, source_target_pairs={{1,0},{2,1},{3,2},{4,3},{5,4},{6,5},{7,6},{8,7},{9,8},{10,9},{11,1... | collective-permute-start | bytes 1572872 | tf_op jit(solution)/shard_map/ppermute | solution.py:22
  62.9 25.1 %collective-permute-start.4 = (f32[2,8,1,32,256]{4,3,2,1,0:T(8,128)S(1)}, f32[2,8,1,32,256]{4,3,2,1,0:T(8,128)S(1)}, u32[]{:S(2)}, u32[]{:S(2)}) collective-permute-start(f32[2,8,1,32,256]{4,3,2,1,0:T(8,128)S(1)} %get-tuple-element.35), channel_id=1, source_target_pairs={{0,1},{1,2},{2,3},{3,4},{4,5},{5,6},{6,7},{7,8},{8,9},{9,10},{10,1... | collective-permute-start | bytes 1572872 | tf_op jit(solution)/shard_map/ppermute | solution.py:20
  67.1 20.9 %collective-permute-start.5 = (f32[2,8,1,32,256]{4,3,2,1,0:T(8,128)S(1)}, f32[2,8,1,32,256]{4,3,2,1,0:T(8,128)S(1)}, u32[]{:S(2)}, u32[]{:S(2)}) collective-permute-start(f32[2,8,1,32,256]{4,3,2,1,0:T(8,128)S(1)} %get-tuple-element.36), channel_id=1, source_target_pairs={{1,0},{2,1},{3,2},{4,3},{5,4},{6,5},{7,6},{8,7},{9,8},{10,9},{11,1... | collective-permute-start | bytes 1572872 | tf_op jit(solution)/shard_map/ppermute | solution.py:22
  91.1 24.0 %collective-permute-start.6 = (f32[2,8,1,32,256]{4,3,2,1,0:T(8,128)S(1)}, f32[2,8,1,32,256]{4,3,2,1,0:T(8,128)S(1)}, u32[]{:S(2)}, u32[]{:S(2)}) collective-permute-start(f32[2,8,1,32,256]{4,3,2,1,0:T(8,128)S(1)} %get-tuple-element.33), channel_id=1, source_target_pairs={{0,1},{1,2},{2,3},{3,4},{4,5},{5,6},{6,7},{7,8},{8,9},{9,10},{10,1... | collective-permute-start | bytes 1572872 | tf_op jit(solution)/shard_map/ppermute | solution.py:20
  95.3 19.9 %collective-permute-start.7 = (f32[2,8,1,32,256]{4,3,2,1,0:T(8,128)S(1)}, f32[2,8,1,32,256]{4,3,2,1,0:T(8,128)S(1)}, u32[]{:S(2)}, u32[]{:S(2)}) collective-permute-start(f32[2,8,1,32,256]{4,3,2,1,0:T(8,128)S(1)} %get-tuple-element.34), channel_id=1, source_target_pairs={{1,0},{2,1},{3,2},{4,3},{5,4},{6,5},{7,6},{8,7},{9,8},{10,9},{11,1... | collective-permute-start | bytes 1572872 | tf_op jit(solution)/shard_map/ppermute | solution.py:22
  120.1 22.0 %all-to-all-start.1 = ((f32[16,2,32,256]{3,1,0,2:T(2,128)}), f32[16,2,32,256]{3,1,0,2:T(2,128)S(1)}, u32[]{:S(2)}, u32[]{:S(2)}) async-start(f32[16,2,32,256]{3,1,0,2:T(2,128)} %copy.36), calls=%async_computation.1 | async-start | bytes 2097152 | tf_op jit(solution)/shard_map/all_to_all | solution.py:129
  127.0 290.7 %all-reduce.7.cloned.1.call-start = ((), (), s32[]{:S(2)}) async-start(), calls=%async_computation.2 | async-start | bytes 131072 | tf_op jit(solution)/shard_map/psum | solution.py:131
  149.9 528.9 %all-reduce.9.cloned.1.call-start = ((), (), s32[]{:S(2)}) async-start(), calls=%async_computation.3 | async-start | bytes 131072 | tf_op jit(solution)/shard_map/psum | solution.py:133
  417.8 5.0 copy-start
  684.6 111.0 %copy-start.1 = (f32[64,256]{1,0:T(8,128)S(1)}, f32[64,256]{1,0:T(8,128)}, u32[]{:S(2)}) copy-start(f32[64,256]{1,0:T(8,128)} %all-reduce.7.cloned.1.call-done) | copy-start | bytes 196612
  684.6 111.0 %copy-start.2 = (f32[64,256]{1,0:T(8,128)S(1)}, f32[64,256]{1,0:T(8,128)}, u32[]{:S(2)}) copy-start(f32[64,256]{1,0:T(8,128)} %all-reduce.9.cloned.1.call-done) | copy-start | bytes 196612
Sparse Core Ops, SparseCore 0:
  150.0 267.6 all-reduce.6
  427.5 251.2 all-reduce.8
where the time goes:
time: 804 us; the launch traced here: 803 us
  waiting for transfers between devices  598 us (74%)
  blocking collectives  94.9 us (12%)
  starting transfers between devices  34.2 us (4%)
  matrix products  23.7 us (3%)
  other arithmetic  23.2 us (3%)
  local copies, waits for them, and re-layouts  15.2 us (2%)
  between operations  14.3 us (2%)
    psum x2, waiting for transfers between devices, local(): lax.psum(products(columns, flat_basis), ('shift', 'space')) * cell_weight  519 us
    psum x1, blocking collectives, local(): lax.psum(products(columns, columns), ('shift', 'space')) * cell_weight  94.9 us
    ppermute x4, waiting for transfers between devices, padded_2(): lax.ppermute(tail, axis, [(i, (i + 1) % count) for i in range(ends)])  69 us
  transfers between devices with their start and end apart: 12, of which 8 were waited for; matrix products, arithmetic and copies ran while one was open for 1% of the time, Pallas kernels for 0%

commit v1 on v0

--- a/solution.py
+++ b/solution.py
@@ -2,11 +2,18 @@
 import jax.numpy as jnp
 from jax import lax
 from jax.sharding import PartitionSpec as P
+from jax.lax import psum
 
 COLS = 8
 SWEEPS = 4
 LOWER_BOUND = 0.1
 UPPER_BOUND = 2.0
+
+
+def _clear_waves(obj):
+    for jj in ("shift", "space"):
+        obj = psum(obj, jj)
+    return obj
 
 
 def padded_2(cells, sides, width):
@@ -128,7 +135,7 @@
     merged = fields.reshape(per_device * COLS, slab_x, full_y, depth)
     regrouped = lax.all_to_all(merged, "shift", split_axis=2, concat_axis=0, tiled=True)
     columns = regrouped.reshape(new_count, slab_x * quarter * depth)
-    first_proj = lax.psum(products(columns, flat_basis), ("shift", "space")) * cell_weight
+    first_proj = _clear_waves(products(columns, flat_basis)) * cell_weight
     columns = columns - matmul(first_proj, flat_basis)
     second_proj = lax.psum(products(columns, flat_basis), ("shift", "space")) * cell_weight
     columns = columns - matmul(second_proj, flat_basis)

time: 804 us -> 1630 us (2.03)
  waiting for transfers between devices: 598 us -> 1430 us
    psum x0 -> x2, waiting for transfers between devices: none -> 1040 us  [_clear_waves(): obj = psum(obj, jj)]
    psum x2 -> x1, waiting for transfers between devices: 519 us -> 313 us  [local(): lax.psum(products(columns, flat_basis), ('shift', 'space')) * cell_weight]
  transfers between devices with their start and end apart: 12 -> 13, of which waited for: 8 -> 9; matrix products, arithmetic and copies ran while one was open for 1% -> 1% of each run, Pallas kernels for 0% -> 0%
where the time goes in v1:
time: 1630 us
  waiting for transfers between devices  1430 us (88%)
  blocking collectives  94.9 us (6%)
  starting transfers between devices  34.2 us (2%)
  matrix products  23.7 us (1%)
  other arithmetic  23.2 us (1%)
    psum x2, waiting for transfers between devices, _clear_waves(): obj = psum(obj, jj)  1040 us
    psum x1, waiting for transfers between devices, local(): lax.psum(products(columns, flat_basis), ('shift', 'space')) * cell_weight  313 us
    psum x1, blocking collectives, local(): lax.psum(products(columns, columns), ('shift', 'space')) * cell_weight  94.9 us
    ppermute x4, waiting for transfers between devices, padded_2(): lax.ppermute(tail, axis, [(i, (i + 1) % count) for i in range(ends)])  69 us
  transfers between devices with their start and end apart: 13, of which 9 were waited for; matrix products, arithmetic and copies ran while one was open for 1% of the time, Pallas kernels for 0%

profile of v1, /device:TPU:1, one launch (start us, length us, event | category | flops | bytes accessed | tf_op | source)
XLA Modules:
  0.0 1633.9 jit_solution(6214768572337846708)
XLA Ops:
  7.2 2.3 slice.133
  9.5 10.4 all-to-all-start
  22.8 10.3 collective-permute-done
  33.4 2.3 all-to-all-done
  36.1 1.9 collective-permute-start.2
  39.2 20.6 %collective-permute-done.2 = f32[2,8,1,32,256]{4,3,2,1,0:T(8,128)S(1)} collective-permute-done((f32[2,8,1,32,256]{4,3,2,1,0:T(8,128)S(1)}, f32[2,8,1,32,256]{4,3,2,1,0:T(8,128)S(1)}, u32[]{:S(2)}, u32[]{:S(2)}) %collective-permute-start.2) | collective-permute-done | bytes 524320 | tf_op jit(solution)/shard_map/ppermute | solution.py:27
  59.8 1.8 select_maximum_fusion.4
  62.9 4.1 collective-permute-start.4
  68.4 19.6 %collective-permute-done.4 = f32[2,8,1,32,256]{4,3,2,1,0:T(8,128)S(1)} collective-permute-done((f32[2,8,1,32,256]{4,3,2,1,0:T(8,128)S(1)}, f32[2,8,1,32,256]{4,3,2,1,0:T(8,128)S(1)}, u32[]{:S(2)}, u32[]{:S(2)}) %collective-permute-start.4) | collective-permute-done | bytes 524320 | tf_op jit(solution)/shard_map/ppermute | solution.py:27
  91.1 4.1 collective-permute-start.6
  96.6 18.6 %collective-permute-done.6 = f32[2,8,1,32,256]{4,3,2,1,0:T(8,128)S(1)} collective-permute-done((f32[2,8,1,32,256]{4,3,2,1,0:T(8,128)S(1)}, f32[2,8,1,32,256]{4,3,2,1,0:T(8,128)S(1)}, u32[]{:S(2)}, u32[]{:S(2)}) %collective-permute-start.6) | collective-permute-done | bytes 524320 | tf_op jit(solution)/shard_map/ppermute | solution.py:27
  120.1 6.9 all-to-all-start.1
  127.0 7.9 copy.46
  135.0 7.2 all-to-all-done.1
  143.1 6.8 fusion.71
  149.9 59.8 %all-reduce.8.cloned.1.call-done = f32[64,256]{1,0:T(8,128)} async-done(((f32[64,256]{1,0:T(8,128)}), f32[64,256]{1,0:T(8,128)}) %all-reduce.8.cloned.1.call-update) | async-done | bytes 65552 | tf_op jit(solution)/shard_map/psum | solution.py:15
  210.0 977.7 %all-reduce.10.cloned.1.call-done = f32[64,256]{1,0:T(8,128)} async-done(((f32[64,256]{1,0:T(8,128)}), f32[64,256]{1,0:T(8,128)}) %all-reduce.10.cloned.1.call-update) | async-done | bytes 65552 | tf_op jit(solution)/shard_map/psum | solution.py:15
  1187.8 5.0 convolution_subtract_fusion.1
  1192.8 4.6 fusion.72
  1197.4 312.5 %all-reduce.12.cloned.1.call-done = f32[64,256]{1,0:T(8,128)} async-done(((f32[64,256]{1,0:T(8,128)}), f32[64,256]{1,0:T(8,128)}) %all-reduce.12.cloned.1.call-update) | async-done | bytes 65552 | tf_op jit(solution)/shard_map/psum | solution.py:140
  1509.9 4.8 convolution_subtract_fusion
  1515.7 94.9 %psum.31 = f32[64,64]{0,1:T(8,128)S(1)} all-reduce(f32[64,64]{0,1:T(8,128)S(1)} %fusion.73), channel_id=1, replica_groups=mesh['shift'=4,'space'=128] {'shift','space'}, use_global_device_ids=true, to_apply=%region_5.6 | all-reduce | flops 4096 | bytes 32768 | tf_op jit(solution)/shard_map/psum | solution.py:142
  1610.7 5.8 cholesky.16
  1618.5 4.9 custom-call.6
  (61 shorter events, 25.0 us)
Async XLA Ops:
  7.2 12.7 copy-start.5
  7.2 12.7 copy-start.4
  7.2 12.7 copy-start.3
  7.2 15.5 copy-start.6
  9.5 26.2 %all-to-all-start = ((f32[64,2,8,256]{3,2,1,0:T(8,128)}), f32[64,2,8,256]{3,2,1,0:T(8,128)S(1)}, u32[]{:S(2)}, u32[]{:S(2)}) async-start(f32[64,2,8,256]{3,2,1,0:T(8,128)} %slice.133), calls=%async_computation | async-start | bytes 2097152 | tf_op jit(solution)/shard_map/all_to_all | solution.py:126
  20.1 13.0 collective-permute-start
  21.4 11.7 collective-permute-start.1
  36.1 23.7 %collective-permute-start.2 = (f32[2,8,1,32,256]{4,3,2,1,0:T(8,128)S(1)}, f32[2,8,1,32,256]{4,3,2,1,0:T(8,128)S(1)}, u32[]{:S(2)}, u32[]{:S(2)}) collective-permute-start(f32[2,8,1,32,256]{4,3,2,1,0:T(8,128)S(1)} %get-tuple-element.37), channel_id=1, source_target_pairs={{0,1},{1,2},{2,3},{3,4},{4,5},{5,6},{6,7},{7,8},{8,9},{9,10},{10,1... | collective-permute-start | bytes 1572872 | tf_op jit(solution)/shard_map/ppermute | solution.py:27
  37.9 21.9 %collective-permute-start.3 = (f32[2,8,1,32,256]{4,3,2,1,0:T(8,128)S(1)}, f32[2,8,1,32,256]{4,3,2,1,0:T(8,128)S(1)}, u32[]{:S(2)}, u32[]{:S(2)}) collective-permute-start(f32[2,8,1,32,256]{4,3,2,1,0:T(8,128)S(1)} %get-tuple-element.38), channel_id=1, source_target_pairs={{1,0},{2,1},{3,2},{4,3},{5,4},{6,5},{7,6},{8,7},{9,8},{10,9},{11,1... | collective-permute-start | bytes 1572872 | tf_op jit(solution)/shard_map/ppermute | solution.py:29
  62.9 25.1 %collective-permute-start.4 = (f32[2,8,1,32,256]{4,3,2,1,0:T(8,128)S(1)}, f32[2,8,1,32,256]{4,3,2,1,0:T(8,128)S(1)}, u32[]{:S(2)}, u32[]{:S(2)}) collective-permute-start(f32[2,8,1,32,256]{4,3,2,1,0:T(8,128)S(1)} %get-tuple-element.35), channel_id=1, source_target_pairs={{0,1},{1,2},{2,3},{3,4},{4,5},{5,6},{6,7},{7,8},{8,9},{9,10},{10,1... | collective-permute-start | bytes 1572872 | tf_op jit(solution)/shard_map/ppermute | solution.py:27
  67.1 20.9 %collective-permute-start.5 = (f32[2,8,1,32,256]{4,3,2,1,0:T(8,128)S(1)}, f32[2,8,1,32,256]{4,3,2,1,0:T(8,128)S(1)}, u32[]{:S(2)}, u32[]{:S(2)}) collective-permute-start(f32[2,8,1,32,256]{4,3,2,1,0:T(8,128)S(1)} %get-tuple-element.36), channel_id=1, source_target_pairs={{1,0},{2,1},{3,2},{4,3},{5,4},{6,5},{7,6},{8,7},{9,8},{10,9},{11,1... | collective-permute-start | bytes 1572872 | tf_op jit(solution)/shard_map/ppermute | solution.py:29
  91.1 24.0 %collective-permute-start.6 = (f32[2,8,1,32,256]{4,3,2,1,0:T(8,128)S(1)}, f32[2,8,1,32,256]{4,3,2,1,0:T(8,128)S(1)}, u32[]{:S(2)}, u32[]{:S(2)}) collective-permute-start(f32[2,8,1,32,256]{4,3,2,1,0:T(8,128)S(1)} %get-tuple-element.33), channel_id=1, source_target_pairs={{0,1},{1,2},{2,3},{3,4},{4,5},{5,6},{6,7},{7,8},{8,9},{9,10},{10,1... | collective-permute-start | bytes 1572872 | tf_op jit(solution)/shard_map/ppermute | solution.py:27
  95.3 19.9 %collective-permute-start.7 = (f32[2,8,1,32,256]{4,3,2,1,0:T(8,128)S(1)}, f32[2,8,1,32,256]{4,3,2,1,0:T(8,128)S(1)}, u32[]{:S(2)}, u32[]{:S(2)}) collective-permute-start(f32[2,8,1,32,256]{4,3,2,1,0:T(8,128)S(1)} %get-tuple-element.34), channel_id=1, source_target_pairs={{1,0},{2,1},{3,2},{4,3},{5,4},{6,5},{7,6},{8,7},{9,8},{10,9},{11,1... | collective-permute-start | bytes 1572872 | tf_op jit(solution)/shard_map/ppermute | solution.py:29
  120.1 22.0 %all-to-all-start.1 = ((f32[16,2,32,256]{3,1,0,2:T(2,128)}), f32[16,2,32,256]{3,1,0,2:T(2,128)S(1)}, u32[]{:S(2)}, u32[]{:S(2)}) async-start(f32[16,2,32,256]{3,1,0,2:T(2,128)} %copy.36), calls=%async_computation.1 | async-start | bytes 2097152 | tf_op jit(solution)/shard_map/all_to_all | solution.py:136
  127.0 82.7 %all-reduce.8.cloned.1.call-start = ((), (), s32[]{:S(2)}) async-start(), calls=%async_computation.2 | async-start | bytes 131072 | tf_op jit(solution)/shard_map/psum | solution.py:15
  149.9 1037.9 %all-reduce.10.cloned.1.call-start = ((), (), s32[]{:S(2)}) async-start(), calls=%async_computation.3 | async-start | bytes 131072 | tf_op jit(solution)/shard_map/psum | solution.py:15
  209.8 1300.1 %all-reduce.12.cloned.1.call-start = ((), (), s32[]{:S(2)}) async-start(), calls=%async_computation.4 | async-start | bytes 131072 | tf_op jit(solution)/shard_map/psum | solution.py:140
  1187.8 5.0 copy-start
  1515.7 111.0 %copy-start.1 = (f32[64,256]{1,0:T(8,128)S(1)}, f32[64,256]{1,0:T(8,128)}, u32[]{:S(2)}) copy-start(f32[64,256]{1,0:T(8,128)} %all-reduce.10.cloned.1.call-done) | copy-start | bytes 196612
  1515.7 111.0 %copy-start.2 = (f32[64,256]{1,0:T(8,128)S(1)}, f32[64,256]{1,0:T(8,128)}, u32[]{:S(2)}) copy-start(f32[64,256]{1,0:T(8,128)} %all-reduce.12.cloned.1.call-done) | copy-start | bytes 196612
Sparse Core Ops, SparseCore 0:
  150.0 59.6 all-reduce.7
  212.9 974.8 all-reduce.9
  1197.5 312.3 all-reduce.11
